TPU v7x, 32 devices: a whole 2x2x4 slice. The times are simulated.
32 devices in a mesh: ctx: 4 (over z), fsdp: 2 (over y), rep: 4 (over x, core).
Axes of the slice: x: 2, y: 2, z: 4, core: 2. Of those that a mesh axis runs over, the one named last changes fastest.
Arguments:
- frames_in: bfloat16 [8, 512, 1024], P('rep', 'ctx', 'fsdp'), parts along dimension 0, may hold values from -6 to 6
- lengths: int32 [8], P('rep'), parts along dimension 0, may hold values from 128 to 512, as said below
- conv_weight: bfloat16 [16, 128, 64, 64], P('fsdp'), may hold values from -0.0625 to 0.0625
- conv_bias: bfloat16 [1024], P('fsdp'), may hold values from -3 to 3
- norm_gain: float32 [1024], replicated, may hold values from 0.1 to 1.9
- norm_shift: float32 [1024], replicated, may hold values from -3 to 3
- w_query: bfloat16 [1024, 512], replicated
- w_key: bfloat16 [1024, 512], replicated
- w_value: bfloat16 [1024, 512], replicated, may hold values from -0.1875 to 0.1875
Outputs:
- hidden: bfloat16 [8, 512, 1024], P('rep', 'ctx', 'fsdp'), parts along dimension 0
- context: bfloat16 [8, 512, 512], P(('rep', 'fsdp'), 'ctx'), parts along dimension 0
There are 4 independent parts, one for each index of `rep`. A program takes and returns all parts, laid end to end along the dimension named above; an argument that names none is the same for every part. Nothing has to cross between parts.
Inputs may be any that keep to these rules, and one draw needn't show every extreme that they name: `lengths`: one recording in every draw has all 512 frames live.
All inputs are finite; a program needn't handle non-finite values.
Results may differ from a plain program's by a relative error of at most 0.012.
Values may be sent and summed in bfloat16 or wider, within the bound.
No kernel may reach another device: no remote copies, remote signals or barrier semaphores. Data moves between devices by JAX's collectives and lax.ppermute only.
A program may use at most 128 MiB of HBM per device.

v0:
```python
import math
import jax
import jax.numpy as jnp
from jax import lax
from jax.sharding import PartitionSpec as P

HD = 64


def padded_2(x, sides, width):
    for axis, dim in sides:
        size, length = (lax.axis_size(axis), x.shape[dim])
        up = [(i, (i + 1) % size) for i in range(size - 1)]
        down = [(j, i) for i, j in up]
        last = lax.slice_in_dim(x, length - width, length, axis=dim)
        first = lax.slice_in_dim(x, 0, width, axis=dim)
        before = lax.ppermute(last, axis, up)
        after = lax.ppermute(first, axis, down)
        x = jnp.concatenate([before, x, after], axis=dim)
    return x


def attend(carry, piece, start, queries, own_length):
    best, total, accum = carry
    keys_part, vals_part = piece
    count = keys_part.shape[0]
    head_count = queries.shape[1]
    keys_part = keys_part.reshape(count, head_count, HD)
    vals_part = vals_part.reshape(count, head_count, HD)
    scores = jnp.einsum(
        "fhd,nhd->fhn", queries, keys_part, preferred_element_type=jnp.float32
    ) / math.sqrt(HD)
    valid = (start + jnp.arange(count, dtype=jnp.int32) < own_length)[None, None, :]
    scores = jnp.where(valid, scores, -1e30)
    fresh = jnp.maximum(best, jnp.max(scores, axis=2))
    weights = jnp.where(valid, jnp.exp(scores - fresh[:, :, None]), 0.0)
    factor = jnp.exp(best - fresh)
    total = total * factor + jnp.sum(weights, axis=2)
    accum = accum * factor[:, :, None] + jnp.einsum(
        "fhn,nhd->fhd", weights.astype(jnp.bfloat16), vals_part, preferred_element_type=jnp.float32
    )
    return (fresh, total, accum)


def start_state(rows, heads_here):
    return (
        jnp.full((rows, heads_here), -1e30, jnp.float32),
        jnp.zeros((rows, heads_here), jnp.float32),
        jnp.zeros((rows, heads_here, HD), jnp.float32),
    )


def blockwise(carry, all_keys, all_vals, queries, own_length, block_rows):
    block_count = all_keys.shape[0] // block_rows

    def block_step(state, index):
        begin = index * block_rows
        piece = (
            lax.dynamic_slice_in_dim(all_keys, begin, block_rows, 0),
            lax.dynamic_slice_in_dim(all_vals, begin, block_rows, 0),
        )
        return (attend(state, piece, begin, queries, own_length), None)

    final, unused = lax.scan(block_step, carry, jnp.arange(block_count, dtype=jnp.int32))
    return final


def finish(final, query_pos, own_length):
    best, total, accum = final
    result = accum / total[:, :, None]
    query_live = (query_pos < own_length)[:, None, None]
    result = jnp.where(query_live, result, 0.0)
    return result.reshape(result.shape[0], result.shape[1] * HD).astype(jnp.bfloat16)


def per_device(
    frames_in, lengths, conv_weight, conv_bias, norm_gain, norm_shift, w_query, w_key, w_value
):
    record_count, frame_rows, channels = frames_in.shape
    ctx_place = lax.axis_index("ctx")
    positions = ctx_place * frame_rows + jnp.arange(frame_rows, dtype=jnp.int32)
    live = positions[None, :] < lengths[:, None]
    masked = jnp.where(live[:, :, None], frames_in, jnp.zeros((), frames_in.dtype))
    groups_here, kernel_width, group_in, group_out = conv_weight.shape
    half_width = kernel_width // 2
    padded = padded_2(masked, (("ctx", 1),), half_width)
    kernel = conv_weight.transpose(1, 2, 0, 3).reshape(
        kernel_width, group_in, groups_here * group_out
    )
    conv_out = lax.conv_general_dilated(
        padded[:, : frame_rows + kernel_width - 1],
        kernel,
        (1,),
        "VALID",
        dimension_numbers=("NWC", "WIO", "NWC"),
        feature_group_count=groups_here,
        preferred_element_type=jnp.float32,
    )
    hidden = (
        masked.astype(jnp.float32)
        + jax.nn.gelu(conv_out + conv_bias.astype(jnp.float32), approximate=False)
    ).astype(jnp.bfloat16)
    record = lax.all_to_all(hidden, "fsdp", split_axis=0, concat_axis=2, tiled=True)
    own_length = lax.dynamic_index_in_dim(lengths, lax.axis_index("fsdp"), 0, keepdims=False)
    flat = record[0].astype(jnp.float32)
    centre = jnp.mean(flat, axis=1, keepdims=True)
    spread = jnp.mean((flat - centre) ** 2, axis=1, keepdims=True)
    normed = ((flat - centre) / jnp.sqrt(spread + 1e-05) * norm_gain + norm_shift).astype(
        jnp.bfloat16
    )
    query_flat = jnp.dot(normed, w_query, preferred_element_type=jnp.float32).astype(jnp.bfloat16)
    key_flat = jnp.dot(normed, w_key, preferred_element_type=jnp.float32).astype(jnp.bfloat16)
    val_flat = jnp.dot(normed, w_value, preferred_element_type=jnp.float32).astype(jnp.bfloat16)
    head_count = query_flat.shape[1] // HD
    queries = query_flat.reshape(frame_rows, head_count, HD)
    block_rows = 4 * frame_rows
    both = lax.all_gather(jnp.concatenate([key_flat, val_flat], axis=1), "ctx", axis=0, tiled=True)
    whole_keys, whole_vals = (both[:, : key_flat.shape[1]], both[:, key_flat.shape[1] :])
    final = blockwise(
        start_state(frame_rows, head_count), whole_keys, whole_vals, queries, own_length, block_rows
    )
    result = finish(final, positions, own_length).reshape(1, frame_rows, head_count * HD)
    return (hidden, result)


def solution(mesh):
    in_specs = (
        P("rep", "ctx", "fsdp"),
        P("rep"),
        P("fsdp", None, None, None),
        P("fsdp"),
        P(),
        P(),
        P(),
        P(),
        P(),
    )
    out_specs = (P("rep", "ctx", "fsdp"), P(("rep", "fsdp"), "ctx", None))
    return jax.shard_map(
        per_device, mesh=mesh, in_specs=in_specs, out_specs=out_specs, check_vma=False
    )
```

profile of v0, /device:TPU:0, one launch (start us, length us, event | category | flops | bytes accessed | tf_op | source)
XLA Modules:
  0.0 142.5 jit_solution(2669789858870461635)
XLA Ops:
  7.2 0.0 copy-start
  7.2 0.0 all-gather.2.cloned.1.call-start
  7.2 1.2 copy.17
  8.4 0.0 copy-start.1
  8.5 0.8 broadcast_compare_fusion
  9.2 0.5 copy-done.8
  9.8 0.1 fusion.36
  9.9 4.9 %collective-permute-start = (bf16[2,64,512]{1,2,0:T(8,128)(2,1)S(1)}, bf16[2,64,512]{1,2,0:T(8,128)(2,1)S(1)}, u32[]{:S(2)}, u32[]{:S(2)}) collective-permute-start(bf16[2,64,512]{1,2,0:T(8,128)(2,1)S(1)} %get-tuple-element.32), channel_id=1, source_target_pairs={{0,8},{8,16},{16,24},{1,9},{9,17},{17,25},{2,10},{10,18},{18,26},{... | collective-permute-start | bytes 393224 | tf_op jit(solution)/shard_map/ppermute | solution.py:17
  14.8 0.0 copy-start.10
  14.9 1.3 collective-permute-start.1
  16.2 24.0 %copy.19 = bf16[8,128,64,64]{3,2,0,1:T(8,128)(2,1)} copy(bf16[8,128,64,64]{1,3,2,0:T(8,128)(2,1)} %param.11) | data formatting | bytes 16777216 | tf_op args[2]
  40.1 0.0 copy-done.10
  40.1 0.6 convert_element_type.59
  40.7 0.0 collective-permute-done
  40.7 0.0 collective-permute-done.1
  40.7 0.3 pad_maximum_fusion
  41.1 2.1 %copy.18 = bf16[2,255,8,64]{3,0,2,1:T(2,128)(2,1)} copy(bf16[2,255,8,64]{1,3,2,0:T(8,128)(2,1)S(1)} %bitcast.62) | data formatting | bytes 1044480 | tf_op jit(solution)/shard_map/slice | solution.py:91
  43.2 41.1 %fusion.37 = f32[2,128,8,64]{3,0,2,1:T(2,128)S(1)} fusion(bf16[2,255,8,64]{3,0,2,1:T(2,128)(2,1)} %copy.18, bf16[8,128,64,64]{3,2,0,1:T(8,128)(2,1)} %copy.19), kind=kOutput, calls=%fused_computation.68 | convolution fusion | flops 2147483648 | bytes 9435136 | tf_op jit(solution)/shard_map/conv_general_dilated | solution.py:90
  84.2 0.0 copy-start.6
  84.3 0.0 copy-start.7
  84.3 0.7 copy.20
  85.0 0.0 copy-start.3
  85.0 1.3 fusion.17
  86.3 7.8 %all_to_all.4 = bf16[2,128,512]{1,2,0:T(8,128)(2,1)S(1)} all-to-all(bf16[2,128,512]{1,2,0:T(8,128)(2,1)S(1)} %fusion.17), channel_id=1, replica_groups=mesh['ctx'=4,'fsdp'=2,'rep'=4] {'fsdp'}, dimensions={0} | all-to-all | bytes 524288 | tf_op jit(solution)/shard_map/all_to_all | solution.py:103
  94.1 0.2 convert_reduce_fusion
  94.2 0.2 fusion.22
  94.4 0.0 copy-start.11
  94.4 0.3 fusion.29
  94.8 0.0 copy-start.4
  94.8 0.3 convolution_convert_fusion.1
  95.1 0.0 copy-done.3
  95.1 0.3 convolution_convert_fusion.2
  95.5 0.7 pad_maximum_fusion.2
  96.2 0.0 all-gather.2.cloned.1.call-update
  96.3 0.6 dynamic_slice.11
  96.8 0.6 iota_compare_fusion
  97.5 0.7 broadcast_compare_fusion.1
  98.2 0.9 copy.25
  99.0 0.3 convolution_convert_fusion
  99.4 0.1 copy.22
  99.5 26.2 %all-gather.2.cloned.1.call-done = bf16[512,1024]{1,0:T(8,128)(2,1)} async-done(((bf16[128,1024]{1,0:T(8,128)(2,1)}), bf16[512,1024]{1,0:T(8,128)(2,1)}) %all-gather.2.cloned.1.call-update) | async-done | bytes 1048592 | tf_op jit(solution)/shard_map/all_gather | solution.py:117
  125.7 2.1 %fusion.35 = (bf16[512,512]{1,0:T(8,128)(2,1)S(1)}, bf16[512,512]{1,0:T(8,128)(2,1)}) fusion(bf16[512,1024]{1,0:T(8,128)(2,1)} %all-gather.2.cloned.1.call-done), kind=kLoop, calls=%fused_computation.66 | loop fusion | bytes 2097152 | tf_op jit(solution)/shard_map/slice | solution.py:118
  127.8 1.0 copy.21
  128.8 1.7 %bitcast_reduce_fusion = (f32[128,8]{0,1:T(8,128)S(1)}, f32[8,512,128]{2,1,0:T(8,128)S(1)}) fusion(pred[512]{0:T(512)(128)(4,1)S(1)} %iota_compare_fusion, bf16[512,8,64]{0,2,1:T(8,128)(2,1)} %bitcast.63, bf16[128,8,64]{0,2,1:T(8,128)(2,1)S(1)} %bitcast.64), kind=kOutput, calls=%fused_computation.1 | convolution fusion | flops 68680704 | bytes 2757120 | tf_op jit(solution)/shard_map/while/body/eval_jaxpr/fhd,nhd->fhn/dot_general | solution.py:30
  130.5 0.6 fusion.2
  131.1 2.1 %copy.23 = bf16[512,512]{0,1:T(8,128)(2,1)} copy(bf16[512,512]{1,0:T(8,128)(2,1)} %get-tuple-element.23) | data formatting | bytes 1048576 | tf_op jit(solution)/shard_map/slice | solution.py:118
  133.1 1.8 %fusion.7 = bf16[128,8,64]{0,2,1:T(8,128)(2,1)S(1)} fusion(bf16[512,8,64]{0,2,1:T(8,128)(2,1)} %bitcast.65, f32[8,512,128]{2,1,0:T(8,128)S(1)} %get-tuple-element.37, f32[128,8]{0,1:T(8,128)S(1)} %broadcast_maximum_fusion, pred[512]{0:T(512)(128)(4,1)S(1)} %iota_compare_fusion, f32[128,8]{0,1:T(8,128)S(1)} %get-tuple-element.35, ...), kind=kOutput, calls=%fused_computation.11 | convolution fusion | flops 69992448 | bytes 2765440 | tf_op jit(solution)/shard_map/while/body/eval_jaxpr/fhn,nhd->fhd/dot_general | solution.py:39
  134.9 0.8 copy.26
  (19 shorter events, 0.1 us)
Async XLA Ops:
  7.2 87.6 %copy-start = (bf16[1024,512]{1,0:T(8,128)(2,1)S(1)}, bf16[1024,512]{1,0:T(8,128)(2,1)}, u32[]{:S(2)}) copy-start(bf16[1024,512]{1,0:T(8,128)(2,1)} %param.17) | copy-start | bytes 3145732
  7.2 118.5 %all-gather.2.cloned.1.call-start = ((), (), s32[]{:S(2)}) async-start(), calls=%async_computation.1 | async-start | bytes 1310720 | tf_op jit(solution)/shard_map/all_gather | solution.py:117
  8.4 31.7 %copy-start.1 = (bf16[2,128,512]{1,2,0:T(8,128)(2,1)}, bf16[2,128,512]{1,2,0:T(8,128)(2,1)S(1)}, u32[]{:S(2)}) copy-start(bf16[2,128,512]{1,2,0:T(8,128)(2,1)S(1)} %copy.17) | copy-start | bytes 786436
  9.2 0.5 copy-start.8
  9.9 30.8 %collective-permute-start = (bf16[2,64,512]{1,2,0:T(8,128)(2,1)S(1)}, bf16[2,64,512]{1,2,0:T(8,128)(2,1)S(1)}, u32[]{:S(2)}, u32[]{:S(2)}) collective-permute-start(bf16[2,64,512]{1,2,0:T(8,128)(2,1)S(1)} %get-tuple-element.32), channel_id=1, source_target_pairs={{0,8},{8,16},{16,24},{1,9},{9,17},{17,25},{2,10},{10,18},{18,26},{... | collective-permute-start | bytes 393224 | tf_op jit(solution)/shard_map/ppermute | solution.py:17
  14.8 25.3 %copy-start.10 = (bf16[512]{0:T(512)(128)(2,1)S(1)}, bf16[512]{0:T(512)(128)(2,1)}, u32[]{:S(2)}) copy-start(bf16[512]{0:T(512)(128)(2,1)} %param.12) | copy-start | bytes 3076
  14.9 25.9 %collective-permute-start.1 = (bf16[2,64,512]{1,2,0:T(8,128)(2,1)S(1)}, bf16[2,64,512]{1,2,0:T(8,128)(2,1)S(1)}, u32[]{:S(2)}, u32[]{:S(2)}) collective-permute-start(bf16[2,64,512]{1,2,0:T(8,128)(2,1)S(1)} %get-tuple-element.33), channel_id=1, source_target_pairs={{8,0},{16,8},{24,16},{9,1},{17,9},{25,17},{10,2},{18,10},{26,18},{... | collective-permute-start | bytes 393224 | tf_op jit(solution)/shard_map/ppermute | solution.py:18
  43.2 41.8 %copy-start.2 = (bf16[2,128,512]{1,2,0:T(8,128)(2,1)S(1)}, bf16[2,128,512]{1,2,0:T(8,128)(2,1)}, u32[]{:S(2)}) copy-start(bf16[2,128,512]{1,2,0:T(8,128)(2,1)} %copy-done.1) | copy-start | bytes 786436
  43.2 41.8 %copy-start.5 = (f32[512]{0:T(512)S(1)}, f32[512]{0:T(512)}, u32[]{:S(2)}) copy-start(f32[512]{0:T(512)} %convert_element_type.59) | copy-start | bytes 6148
  43.2 41.9 %copy-start.9 = (pred[2,128]{1,0:T(4,128)(4,1)S(1)}, pred[2,128]{1,0:T(4,128)(4,1)}, u32[]{:S(2)}) copy-start(pred[2,128]{1,0:T(4,128)(4,1)} %copy-done.8) | copy-start | bytes 772
  84.2 10.1 %copy-start.6 = (f32[1024]{0:T(1024)S(1)}, f32[1024]{0:T(1024)}, u32[]{:S(2)}) copy-start(f32[1024]{0:T(1024)} %param.14) | copy-start | bytes 12292
  84.3 10.1 %copy-start.7 = (f32[1024]{0:T(1024)S(1)}, f32[1024]{0:T(1024)}, u32[]{:S(2)}) copy-start(f32[1024]{0:T(1024)} %param.13) | copy-start | bytes 12292
  85.0 10.1 %copy-start.3 = (bf16[1024,512]{1,0:T(8,128)(2,1)S(1)}, bf16[1024,512]{1,0:T(8,128)(2,1)}, u32[]{:S(2)}) copy-start(bf16[1024,512]{1,0:T(8,128)(2,1)} %param.16) | copy-start | bytes 3145732
  94.4 1.9 %copy-start.11 = (s32[2]{0:T(128)S(1)}, s32[2]{0:T(128)}, u32[]{:S(2)}) copy-start(s32[2]{0:T(128)} %param.10) | copy-start | bytes 28
  94.8 4.3 %copy-start.4 = (bf16[1024,512]{1,0:T(8,128)(2,1)S(1)}, bf16[1024,512]{1,0:T(8,128)(2,1)}, u32[]{:S(2)}) copy-start(bf16[1024,512]{1,0:T(8,128)(2,1)} %param.15) | copy-start | bytes 3145732
Sparse Core Ops, SparseCore 0:
  96.4 29.2 all-gather.1
where the time goes:
time: 143 us
  matrix products  45.5 us (32%)
  local copies, waits for them, and re-layouts  36.2 us (25%)
  waiting for transfers between devices  26.2 us (18%)
  between operations  14.3 us (10%)
  blocking collectives  7.76 us (5%)
  starting transfers between devices  6.27 us (4%)
  other arithmetic  6.24 us (4%)
    conv_general_dilated x1, matrix products, per_device(): lax.conv_general_dilated(padded[:, :frame_rows + kernel_width - 1], kerne...  41.1 us
    unnamed x28, local copies, waits for them, and re-layouts  27.4 us
    all_gather x1, waiting for transfers between devices, per_device(): lax.all_gather(jnp.concatenate([key_flat, val_flat], axis=1), 'ctx', axis...  26.2 us
    all_to_all x1, blocking collectives, per_device(): lax.all_to_all(hidden, 'fsdp', split_axis=0, concat_axis=2, tiled=True)  7.76 us
    ppermute x1, starting transfers between devices, padded_2(): before = lax.ppermute(last, axis, up)  4.94 us
    slice x2, local copies, waits for them, and re-layouts, per_device(): both[:, :key_flat.shape[1]]  3.1 us
  transfers between devices with their start and end apart: 3, of which 1 were waited for; matrix products, arithmetic and copies ran while one was open for 19% of the time, Pallas kernels for 0%

commit v1 on v0

--- a/solution.py
+++ b/solution.py
@@ -1,3 +1,4 @@
+import functools
 import math
 import jax
 import jax.numpy as jnp
@@ -5,6 +6,23 @@
 from jax.sharding import PartitionSpec as P
 
 HD = 64
+
+
+def number_the_hubs(work_x, comm_axis):
+    parts_n = lax.psum(1, comm_axis)
+    block_list = tuple(((dev_j, (dev_j + 1) % parts_n) for dev_j in range(parts_n)))
+    then, ready = ([work_x], [work_x])
+    bank = tuple(((dev_j, (dev_j - 1) % parts_n) for dev_j in range(parts_n)))
+    for _ in range(parts_n // 2):
+        then.append(lax.ppermute(then[-1], comm_axis, block_list))
+    for _ in range((parts_n - 1) // 2):
+        ready.append(lax.ppermute(ready[-1], comm_axis, bank))
+    z_new = jnp.concatenate([*then[::-1], *ready[1:]], 0)
+    base_arr = jnp.roll(z_new, (lax.axis_index(comm_axis) - parts_n // 2) * work_x.shape[0], 0)
+    return base_arr
+
+
+start_shards_all = functools.partial(number_the_hubs, comm_axis="ctx")
 
 
 def padded_2(x, sides, width):
@@ -114,7 +132,7 @@
     head_count = query_flat.shape[1] // HD
     queries = query_flat.reshape(frame_rows, head_count, HD)
     block_rows = 4 * frame_rows
-    both = lax.all_gather(jnp.concatenate([key_flat, val_flat], axis=1), "ctx", axis=0, tiled=True)
+    both = start_shards_all(jnp.concatenate([key_flat, val_flat], axis=1))
     whole_keys, whole_vals = (both[:, : key_flat.shape[1]], both[:, key_flat.shape[1] :])
     final = blockwise(
         start_state(frame_rows, head_count), whole_keys, whole_vals, queries, own_length, block_rows

time: 143 us -> 120 us (0.84)
  waiting for transfers between devices: 26.2 us -> 10.3 us
  between operations: 14.3 us -> 1 us
  starting transfers between devices: 6.27 us -> 12.8 us
    all_gather x1 -> x0, waiting for transfers between devices: 26.2 us -> none  [per_device(): lax.all_gather(jnp.concatenate([key_flat, val_flat], axis=1), 'ctx', axis...]
    ppermute x0 -> x3, waiting for transfers between devices: none -> 10.3 us  [the longest x2 7.83 us: number_the_hubs(): then.append(lax.ppermute(then[-1], comm_axis, block_list))]
    ppermute x0 -> x3, starting transfers between devices: none -> 6.53 us  [the longest x1 3.82 us: number_the_hubs(): ready.append(lax.ppermute(ready[-1], comm_axis, bank))]
    unnamed x28 -> x35, local copies, waits for them, and re-layouts: 27.4 us -> 27.5 us
  transfers between devices with their start and end apart: 3 -> 5, of which waited for: 1 -> 3; matrix products, arithmetic and copies ran while one was open for 19% -> 25% of each run, Pallas kernels for 0% -> 0%
where the time goes in v1:
time: 120 us
  matrix products  46.2 us (38%)
  local copies, waits for them, and re-layouts  36 us (30%)
  starting transfers between devices  12.8 us (11%)
  waiting for transfers between devices  10.3 us (9%)
  blocking collectives  7.76 us (6%)
  other arithmetic  5.56 us (5%)
    conv_general_dilated x1, matrix products, per_device(): lax.conv_general_dilated(padded[:, :frame_rows + kernel_width - 1], kerne...  41.1 us
    unnamed x35, local copies, waits for them, and re-layouts  27.5 us
    ppermute x2, waiting for transfers between devices, number_the_hubs(): then.append(lax.ppermute(then[-1], comm_axis, block_list))  7.83 us
    all_to_all x1, blocking collectives, per_device(): lax.all_to_all(hidden, 'fsdp', split_axis=0, concat_axis=2, tiled=True)  7.76 us
    ppermute x1, starting transfers between devices, padded_2(): before = lax.ppermute(last, axis, up)  4.94 us
    ppermute x1, starting transfers between devices, number_the_hubs(): ready.append(lax.ppermute(ready[-1], comm_axis, bank))  3.82 us
    ppermute x2, starting transfers between devices, number_the_hubs(): then.append(lax.ppermute(then[-1], comm_axis, block_list))  2.71 us
    ppermute x1, waiting for transfers between devices, number_the_hubs(): ready.append(lax.ppermute(ready[-1], comm_axis, bank))  2.48 us
  transfers between devices with their start and end apart: 5, of which 3 were waited for; matrix products, arithmetic and copies ran while one was open for 25% of the time, Pallas kernels for 0%

profile of v1, /device:TPU:0, one launch (start us, length us, event | category | flops | bytes accessed | tf_op | source)
XLA Modules:
  0.0 119.6 jit_solution(3163766439176948879)
XLA Ops:
  0.6 0.0 copy-start
  0.7 1.2 %copy.17 = bf16[2,128,512]{1,2,0:T(8,128)(2,1)S(1)} copy(bf16[2,128,512]{2,1,0:T(8,128)(2,1)} %param.9) | data formatting | bytes 524288 | tf_op args[0]
  1.9 0.0 copy-start.1
  1.9 0.8 broadcast_compare_fusion
  2.6 0.6 copy-done.9
  3.2 0.1 fusion.35
  3.4 4.9 %collective-permute-start = (bf16[2,64,512]{1,2,0:T(8,128)(2,1)S(1)}, bf16[2,64,512]{1,2,0:T(8,128)(2,1)S(1)}, u32[]{:S(2)}, u32[]{:S(2)}) collective-permute-start(bf16[2,64,512]{1,2,0:T(8,128)(2,1)S(1)} %get-tuple-element.32), channel_id=1, source_target_pairs={{0,8},{8,16},{16,24},{1,9},{9,17},{17,25},{2,10},{10,18},{18,26},{... | collective-permute-start | bytes 393224 | tf_op jit(solution)/shard_map/ppermute | solution.py:35
  8.3 0.0 copy-start.11
  8.3 1.3 %collective-permute-start.1 = (bf16[2,64,512]{1,2,0:T(8,128)(2,1)S(1)}, bf16[2,64,512]{1,2,0:T(8,128)(2,1)S(1)}, u32[]{:S(2)}, u32[]{:S(2)}) collective-permute-start(bf16[2,64,512]{1,2,0:T(8,128)(2,1)S(1)} %get-tuple-element.33), channel_id=1, source_target_pairs={{8,0},{16,8},{24,16},{9,1},{17,9},{25,17},{10,2},{18,10},{26,18},{... | collective-permute-start | bytes 393224 | tf_op jit(solution)/shard_map/ppermute | solution.py:36
  9.6 23.9 %copy.19 = bf16[8,128,64,64]{3,2,0,1:T(8,128)(2,1)} copy(bf16[8,128,64,64]{1,3,2,0:T(8,128)(2,1)} %param.11) | data formatting | bytes 16777216 | tf_op args[2]
  33.6 0.0 copy-done.11
  33.6 0.6 convert_element_type.59
  34.2 0.0 collective-permute-done
  34.2 0.0 collective-permute-done.1
  34.2 0.3 pad_maximum_fusion
  34.5 2.1 %copy.18 = bf16[2,255,8,64]{3,0,2,1:T(2,128)(2,1)} copy(bf16[2,255,8,64]{1,3,2,0:T(8,128)(2,1)S(1)} %bitcast.62) | data formatting | bytes 1044480 | tf_op jit(solution)/shard_map/slice | solution.py:109
  36.6 41.1 %fusion.36 = f32[2,128,8,64]{3,0,2,1:T(2,128)S(1)} fusion(bf16[2,255,8,64]{3,0,2,1:T(2,128)(2,1)} %copy.18, bf16[8,128,64,64]{3,2,0,1:T(8,128)(2,1)} %copy.19), kind=kOutput, calls=%fused_computation.76 | convolution fusion | flops 2147483648 | bytes 9435136 | tf_op jit(solution)/shard_map/conv_general_dilated | solution.py:108
  77.7 0.0 copy-start.7
  77.7 0.0 copy-start.8
  77.7 0.7 copy.20
  78.5 0.0 copy-start.3
  78.5 1.3 %fusion.17 = bf16[2,128,512]{1,2,0:T(8,128)(2,1)S(1)} fusion(f32[2,128,8,64]{1,3,2,0:T(8,128)S(1)} %copy.20, f32[512]{0:T(512)S(1)} %copy-done.6, bf16[2,128,512]{1,2,0:T(8,128)(2,1)S(1)} %copy-done.2, pred[2,128]{1,0:T(4,128)(4,1)S(1)} %copy-done.10), kind=kLoop, calls=%fused_computation.24 | loop fusion | flops 9043968 | bytes 1050880 | tf_op jit(solution)/shard_map/convert_element_type | solution.py:120
  79.7 7.8 %all_to_all.4 = bf16[2,128,512]{1,2,0:T(8,128)(2,1)S(1)} all-to-all(bf16[2,128,512]{1,2,0:T(8,128)(2,1)S(1)} %fusion.17), channel_id=1, replica_groups=mesh['ctx'=4,'fsdp'=2,'rep'=4] {'fsdp'}, dimensions={0} | all-to-all | bytes 524288 | tf_op jit(solution)/shard_map/all_to_all | solution.py:121
  87.5 0.2 convert_reduce_fusion
  87.7 0.2 fusion.22
  87.8 0.3 fusion.29
  88.2 0.0 copy-start.4
  88.2 0.3 convolution_convert_fusion.1
  88.6 0.3 convolution_convert_fusion.2
  88.9 2.7 %collective-permute-start.2 = (bf16[128,1024]{1,0:T(8,128)(2,1)S(1)}, bf16[128,1024]{1,0:T(8,128)(2,1)S(1)}, u32[]{:S(2)}, u32[]{:S(2)}) collective-permute-start(bf16[128,1024]{1,0:T(8,128)(2,1)S(1)} %pad_maximum_fusion.2), channel_id=1, source_target_pairs={{0,8},{8,16},{16,24},{24,0},{1,9},{9,17},{17,25},{25,1},{2,10},{10... | collective-permute-start | bytes 786440 | tf_op jit(solution)/shard_map/ppermute | solution.py:17
  91.7 0.6 dynamic_slice.15
  92.2 0.6 iota_compare_fusion
  92.9 5.2 %collective-permute-done.2 = bf16[128,1024]{1,0:T(8,128)(2,1)S(1)} collective-permute-done((bf16[128,1024]{1,0:T(8,128)(2,1)S(1)}, bf16[128,1024]{1,0:T(8,128)(2,1)S(1)}, u32[]{:S(2)}, u32[]{:S(2)}) %collective-permute-start.2) | collective-permute-done | bytes 262176 | tf_op jit(solution)/shard_map/ppermute | solution.py:17
  98.1 0.0 collective-permute-start.3
  98.1 0.7 broadcast_compare_fusion.1
  98.8 0.9 copy.25
  99.6 3.8 %collective-permute-start.4 = (bf16[128,1024]{1,0:T(8,128)(2,1)}, bf16[128,1024]{1,0:T(8,128)(2,1)S(1)}, u32[]{:S(2)}, u32[]{:S(2)}) collective-permute-start(bf16[128,1024]{1,0:T(8,128)(2,1)} %copy-done.5), channel_id=1, source_target_pairs={{0,24},{8,0},{16,8},{24,16},{1,25},{9,1},{17,9},{25,17},{2,26},{10... | collective-permute-start | bytes 786440 | tf_op jit(solution)/shard_map/ppermute | solution.py:19
  103.4 1.0 convolution_convert_fusion
  104.4 1.0 copy.22
  105.4 2.7 %collective-permute-done.3 = bf16[128,1024]{1,0:T(8,128)(2,1)S(1)} collective-permute-done((bf16[128,1024]{1,0:T(8,128)(2,1)S(1)}, bf16[128,1024]{1,0:T(8,128)(2,1)S(1)}, u32[]{:S(2)}, u32[]{:S(2)}) %collective-permute-start.3) | collective-permute-done | bytes 262176 | tf_op jit(solution)/shard_map/ppermute | solution.py:17
  108.2 2.5 %collective-permute-done.4 = bf16[128,1024]{1,0:T(8,128)(2,1)S(1)} collective-permute-done((bf16[128,1024]{1,0:T(8,128)(2,1)}, bf16[128,1024]{1,0:T(8,128)(2,1)S(1)}, u32[]{:S(2)}, u32[]{:S(2)}) %collective-permute-start.4) | collective-permute-done | bytes 262176 | tf_op jit(solution)/shard_map/ppermute | solution.py:19
  110.8 0.9 constant_dynamic-slice_fusion
  111.7 1.0 copy.21
  112.7 1.7 %bitcast_reduce_fusion = (f32[128,8]{0,1:T(8,128)S(1)}, f32[8,512,128]{2,1,0:T(8,128)S(1)}) fusion(pred[512]{0:T(512)(128)(4,1)S(1)} %iota_compare_fusion, bf16[512,8,64]{0,2,1:T(8,128)(2,1)} %bitcast.63, bf16[128,8,64]{0,2,1:T(8,128)(2,1)S(1)} %bitcast.64), kind=kOutput, calls=%fused_computation.1 | convolution fusion | flops 68680704 | bytes 2757120 | tf_op jit(solution)/shard_map/while/body/eval_jaxpr/fhd,nhd->fhn/dot_general | solution.py:48
  114.4 0.6 fusion.2
  115.0 2.0 %copy.23 = bf16[512,512]{0,1:T(8,128)(2,1)} copy(bf16[512,512]{1,0:T(8,128)(2,1)} %get-tuple-element.23) | data formatting | bytes 1048576 | tf_op jit(solution)/shard_map/slice | solution.py:136
  117.0 1.8 %fusion.7 = bf16[128,8,64]{0,2,1:T(8,128)(2,1)S(1)} fusion(bf16[512,8,64]{0,2,1:T(8,128)(2,1)} %bitcast.65, f32[8,512,128]{2,1,0:T(8,128)S(1)} %get-tuple-element.37, f32[128,8]{0,1:T(8,128)S(1)} %broadcast_maximum_fusion, pred[512]{0:T(512)(128)(4,1)S(1)} %iota_compare_fusion, f32[128,8]{0,1:T(8,128)S(1)} %get-tuple-element.35, ...), kind=kOutput, calls=%fused_computation.11 | convolution fusion | flops 69992448 | bytes 2765440 | tf_op jit(solution)/shard_map/while/body/eval_jaxpr/fhn,nhd->fhd/dot_general | solution.py:57
  118.8 0.8 copy.26
  (32 shorter events, 0.3 us)
Async XLA Ops:
  0.6 87.6 %copy-start = (bf16[1024,512]{1,0:T(8,128)(2,1)S(1)}, bf16[1024,512]{1,0:T(8,128)(2,1)}, u32[]{:S(2)}) copy-start(bf16[1024,512]{1,0:T(8,128)(2,1)} %param.17) | copy-start | bytes 3145732
  1.9 31.7 %copy-start.1 = (bf16[2,128,512]{1,2,0:T(8,128)(2,1)}, bf16[2,128,512]{1,2,0:T(8,128)(2,1)S(1)}, u32[]{:S(2)}) copy-start(bf16[2,128,512]{1,2,0:T(8,128)(2,1)S(1)} %copy.17) | copy-start | bytes 786436
  2.6 0.6 copy-start.9
  3.4 30.8 %collective-permute-start = (bf16[2,64,512]{1,2,0:T(8,128)(2,1)S(1)}, bf16[2,64,512]{1,2,0:T(8,128)(2,1)S(1)}, u32[]{:S(2)}, u32[]{:S(2)}) collective-permute-start(bf16[2,64,512]{1,2,0:T(8,128)(2,1)S(1)} %get-tuple-element.32), channel_id=1, source_target_pairs={{0,8},{8,16},{16,24},{1,9},{9,17},{17,25},{2,10},{10,18},{18,26},{... | collective-permute-start | bytes 393224 | tf_op jit(solution)/shard_map/ppermute | solution.py:35
  8.3 25.3 %copy-start.11 = (bf16[512]{0:T(512)(128)(2,1)S(1)}, bf16[512]{0:T(512)(128)(2,1)}, u32[]{:S(2)}) copy-start(bf16[512]{0:T(512)(128)(2,1)} %param.12) | copy-start | bytes 3076
  8.3 25.8 %collective-permute-start.1 = (bf16[2,64,512]{1,2,0:T(8,128)(2,1)S(1)}, bf16[2,64,512]{1,2,0:T(8,128)(2,1)S(1)}, u32[]{:S(2)}, u32[]{:S(2)}) collective-permute-start(bf16[2,64,512]{1,2,0:T(8,128)(2,1)S(1)} %get-tuple-element.33), channel_id=1, source_target_pairs={{8,0},{16,8},{24,16},{9,1},{17,9},{25,17},{10,2},{18,10},{26,18},{... | collective-permute-start | bytes 393224 | tf_op jit(solution)/shard_map/ppermute | solution.py:36
  36.6 41.8 %copy-start.2 = (bf16[2,128,512]{1,2,0:T(8,128)(2,1)S(1)}, bf16[2,128,512]{1,2,0:T(8,128)(2,1)}, u32[]{:S(2)}) copy-start(bf16[2,128,512]{1,2,0:T(8,128)(2,1)} %copy-done.1) | copy-start | bytes 786436
  36.6 41.8 %copy-start.6 = (f32[512]{0:T(512)S(1)}, f32[512]{0:T(512)}, u32[]{:S(2)}) copy-start(f32[512]{0:T(512)} %convert_element_type.59) | copy-start | bytes 6148
  36.6 41.9 %copy-start.10 = (pred[2,128]{1,0:T(4,128)(4,1)S(1)}, pred[2,128]{1,0:T(4,128)(4,1)}, u32[]{:S(2)}) copy-start(pred[2,128]{1,0:T(4,128)(4,1)} %copy-done.9) | copy-start | bytes 772
  77.7 10.2 %copy-start.7 = (f32[1024]{0:T(1024)S(1)}, f32[1024]{0:T(1024)}, u32[]{:S(2)}) copy-start(f32[1024]{0:T(1024)} %param.14) | copy-start | bytes 12292
  77.7 10.1 %copy-start.8 = (f32[1024]{0:T(1024)S(1)}, f32[1024]{0:T(1024)}, u32[]{:S(2)}) copy-start(f32[1024]{0:T(1024)} %param.13) | copy-start | bytes 12292
  78.5 10.1 %copy-start.3 = (bf16[1024,512]{1,0:T(8,128)(2,1)S(1)}, bf16[1024,512]{1,0:T(8,128)(2,1)}, u32[]{:S(2)}) copy-start(bf16[1024,512]{1,0:T(8,128)(2,1)} %param.16) | copy-start | bytes 3145732
  87.7 4.0 %copy-start.12 = (s32[2]{0:T(128)S(1)}, s32[2]{0:T(128)}, u32[]{:S(2)}) copy-start(s32[2]{0:T(128)} %param.10) | copy-start | bytes 28
  88.2 15.2 %copy-start.4 = (bf16[1024,512]{1,0:T(8,128)(2,1)S(1)}, bf16[1024,512]{1,0:T(8,128)(2,1)}, u32[]{:S(2)}) copy-start(bf16[1024,512]{1,0:T(8,128)(2,1)} %param.15) | copy-start | bytes 3145732
  88.9 4.0 %copy-start.5 = (bf16[128,1024]{1,0:T(8,128)(2,1)}, bf16[128,1024]{1,0:T(8,128)(2,1)S(1)}, u32[]{:S(2)}) copy-start(bf16[128,1024]{1,0:T(8,128)(2,1)S(1)} %pad_maximum_fusion.2) | copy-start | bytes 786436
  88.9 9.1 %collective-permute-start.2 = (bf16[128,1024]{1,0:T(8,128)(2,1)S(1)}, bf16[128,1024]{1,0:T(8,128)(2,1)S(1)}, u32[]{:S(2)}, u32[]{:S(2)}) collective-permute-start(bf16[128,1024]{1,0:T(8,128)(2,1)S(1)} %pad_maximum_fusion.2), channel_id=1, source_target_pairs={{0,8},{8,16},{16,24},{24,0},{1,9},{9,17},{17,25},{25,1},{2,10},{10... | collective-permute-start | bytes 786440 | tf_op jit(solution)/shard_map/ppermute | solution.py:17
  98.1 10.0 %collective-permute-start.3 = (bf16[128,1024]{1,0:T(8,128)(2,1)S(1)}, bf16[128,1024]{1,0:T(8,128)(2,1)S(1)}, u32[]{:S(2)}, u32[]{:S(2)}) collective-permute-start(bf16[128,1024]{1,0:T(8,128)(2,1)S(1)} %collective-permute-done.2), channel_id=1, source_target_pairs={{0,8},{8,16},{16,24},{24,0},{1,9},{9,17},{17,25},{25,1},{2,10},{10... | collective-permute-start | bytes 786440 | tf_op jit(solution)/shard_map/ppermute | solution.py:17
  99.6 11.1 %collective-permute-start.4 = (bf16[128,1024]{1,0:T(8,128)(2,1)}, bf16[128,1024]{1,0:T(8,128)(2,1)S(1)}, u32[]{:S(2)}, u32[]{:S(2)}) collective-permute-start(bf16[128,1024]{1,0:T(8,128)(2,1)} %copy-done.5), channel_id=1, source_target_pairs={{0,24},{8,0},{16,8},{24,16},{1,25},{9,1},{17,9},{25,17},{2,26},{10... | collective-permute-start | bytes 786440 | tf_op jit(solution)/shard_map/ppermute | solution.py:19
